TPU v7x, 32 devices: a whole 2x2x4 slice. The times are simulated.
32 devices in a mesh: circ: 4 (over z), normal: 2 (over y), span: 4 (over x, core).
Axes of the slice: x: 2, y: 2, z: 4, core: 2. Of those that a mesh axis runs over, the one named last changes fastest.
Arguments:
- adjoint: float32 [5, 16, 32, 512], P(None, 'span', 'normal', 'circ'), may hold values from -6 to 6
- objective_grad: float32 [5, 16, 32, 512], P(None, 'span', 'normal', 'circ'), may hold values from -6 to 6
- face_weights: float32 [3, 16, 32, 512], P(None, 'span', 'normal', 'circ'), may hold values from 0.2 to 2
- owner_jac: float32 [3, 5, 5], replicated, may hold values from -2.5 to 2.5
- neighbor_jac: float32 [3, 5, 5], replicated, may hold values from -2.5 to 2.5
- coupling: float32 [3, 5], replicated, may hold values from -2.5 to 2.5
- stiffness: float32 [16, 32, 512], P('span', 'normal', 'circ'), may hold values from 0.3 to 3
- wall_kernel: float32 [16, 32, 512], P('span', 'normal', 'circ'), may hold values from -0.25 to 0.25
- panel_owner: int32 [16, 512], P('span', 'circ'), may hold values from 0 to 511, as said below
Outputs:
- adjoint_residual: float32 [5, 16, 32, 512], P(None, 'span', 'normal', 'circ')
- mesh_adjoint: float32 [3, 16, 32, 512], P(None, 'span', 'normal', 'circ')
- panel_sens: float32 [3, 512], P(None, 'span')
Inputs may be any that keep to these rules, and one draw needn't show every extreme that they name: `panel_owner`: the panel of a wall face at station k is owned by span index k // 4 or the one beside it; panels hold ragged numbers of faces.
All inputs are finite; a program needn't handle non-finite values.
Results may differ from a plain program's by a relative error of at most 0.00011.
Values sent between devices are 32-bit elements; how exact they have to be, the bound alone decides.
No kernel may reach another device: no remote copies, remote signals or barrier semaphores. Data moves between devices by JAX's collectives and lax.ppermute only.
A program may use at most 64 MiB of HBM per device.

v0:
```python
import jax
import jax.numpy as jnp
from jax import lax
from jax.sharding import PartitionSpec as P

PANEL_DEV = 128
SWEEPS = 4


def padded_2(array, sides, width, wrap):
    for axis, dim in sides:
        peers, length = (lax.axis_size(axis), array.shape[dim])
        up = [(i, (i + 1) % peers) for i in range(peers if wrap else peers - 1)]
        down = [(j, i) for i, j in up]
        last = lax.slice_in_dim(array, length - width, length, axis=dim)
        initial = lax.slice_in_dim(array, 0, width, axis=dim)
        before = lax.ppermute(last, axis, up)
        after = lax.ppermute(initial, axis, down)
        array = jnp.concatenate([before, array, after], axis=dim)
    return array


def neighbor_sum(padded):
    total = padded[:, 2:, 1:-1, 1:-1] + padded[:, :-2, 1:-1, 1:-1]
    total = total + padded[:, 1:-1, 2:, 1:-1] + padded[:, 1:-1, :-2, 1:-1]
    return total + padded[:, 1:-1, 1:-1, 2:] + padded[:, 1:-1, 1:-1, :-2]


def inner(field):
    return field[:, 1:-1, 1:-1, 1:-1]


def flux_transpose(padded, owner_jac, neighbor_jac):
    psi = padded[:5]
    weights = padded[5:]
    center = inner(psi)
    total = jnp.zeros_like(center)
    for direction in range(3):
        lower = [slice(None), slice(1, -1), slice(1, -1), slice(1, -1)]
        upper = [slice(None), slice(1, -1), slice(1, -1), slice(1, -1)]
        lower[direction + 1] = slice(0, -2)
        upper[direction + 1] = slice(2, None)
        w_here = weights[direction, 1:-1, 1:-1, 1:-1]
        w_lower = weights[direction][tuple(lower[1:])]
        up_term = w_here[None] * (center - psi[tuple(upper)])
        down_term = w_lower[None] * (psi[tuple(lower)] - center)
        total = total + jnp.einsum(
            "uv,ukji->vkji", owner_jac[direction], up_term, precision=lax.Precision.HIGHEST
        )
        total = total + jnp.einsum(
            "uv,ukji->vkji", neighbor_jac[direction], down_term, precision=lax.Precision.HIGHEST
        )
    return total


def relax(mesh_pad, stiff_pad, force_pad):
    weighted = stiff_pad[None] * mesh_pad
    stiff_in = stiff_pad[1:-1, 1:-1, 1:-1]
    diag_term = 6.0 * stiff_in + 1.0
    mesh_in = inner(mesh_pad)
    return (
        mesh_in
        + 0.8
        * (inner(force_pad) - diag_term[None] * mesh_in + neighbor_sum(weighted))
        / diag_term[None]
    )


def run_sweeps(stiff_pad, force_pad):
    mesh_pad = 0.8 * force_pad / (6.0 * stiff_pad[None] + 1.0)
    for sweep in range(1, SWEEPS):
        mesh_pad = relax(mesh_pad, stiff_pad, force_pad)
        stiff_pad = stiff_pad[1:-1, 1:-1, 1:-1]
        force_pad = inner(force_pad)
    return mesh_pad


def on_device(
    adjoint,
    objective_grad,
    face_weights,
    owner_jac,
    neighbor_jac,
    coupling,
    stiffness,
    wall_kernel,
    panel_owner,
):
    stacked = jnp.concatenate([adjoint, face_weights], axis=0)
    beside_all = padded_2(stacked, (("circ", 3),), 1, True)
    padded = padded_2(beside_all, (("normal", 2), ("span", 1)), 1, False)
    residual = flux_transpose(padded, owner_jac, neighbor_jac) + adjoint - objective_grad
    forcing = jnp.einsum("mv,vkji->mkji", coupling, residual, precision=lax.Precision.HIGHEST)
    margin = SWEEPS - 1
    joined = jnp.concatenate([stiffness[None], forcing], axis=0)
    cycle_pad = padded_2(joined, (("circ", 3),), margin, True)
    full_pad = padded_2(cycle_pad, (("normal", 2), ("span", 1)), margin, False)
    mesh = run_sweeps(full_pad[0], full_pad[1:])
    wall_sens = jnp.sum(wall_kernel[None] * mesh, axis=2)
    panel_count = PANEL_DEV * lax.axis_size("span")
    onehot = (
        panel_owner[:, :, None] == jnp.arange(panel_count, dtype=jnp.int32)[None, None, :]
    ).astype(jnp.float32)
    terms = jnp.einsum("mki,kip->mp", wall_sens, onehot, precision=lax.Precision.HIGHEST)
    total = lax.psum(terms, ("circ", "normal", "span"))
    panels = lax.dynamic_slice_in_dim(total, lax.axis_index("span") * PANEL_DEV, PANEL_DEV, 1)
    return (residual, mesh, panels)


def solution(mesh):
    placed = (
        P(None, "span", "normal", "circ"),
        P(None, "span", "normal", "circ"),
        P(None, "span", "normal", "circ"),
        P(),
        P(),
        P(),
        P("span", "normal", "circ"),
        P("span", "normal", "circ"),
        P("span", "circ"),
    )
    return jax.shard_map(
        on_device,
        mesh=mesh,
        in_specs=placed,
        out_specs=(
            P(None, "span", "normal", "circ"),
            P(None, "span", "normal", "circ"),
            P(None, "span"),
        ),
        check_vma=False,
    )
```

profile of v0, /device:TPU:14, one launch (start us, length us, event | category | flops | bytes accessed | tf_op | source)
XLA Modules:
  0.0 115.0 jit_solution(1528439476088058492)
XLA Ops:
  0.6 0.0 copy-start
  0.7 1.0 constant_dynamic-update-slice_fusion.1
  1.6 0.1 fusion.35
  1.8 1.6 %collective-permute-start = (f32[8,4,16,1]{3,2,1,0:T(8,128)S(1)}, f32[8,4,16,1]{3,2,1,0:T(8,128)S(1)}, u32[]{:S(2)}, u32[]{:S(2)}) collective-permute-start(f32[8,4,16,1]{3,2,1,0:T(8,128)S(1)} %get-tuple-element.32), channel_id=1, source_target_pairs={{0,8},{8,16},{16,24},{24,0},{1,9},{9,17},{17,25},{25,1},{2,10},{10... | collective-permute-start | bytes 6152 | tf_op jit(solution)/shard_map/ppermute | solution.py:17
  3.4 0.4 collective-permute-start.1
  3.9 7.2 %collective-permute-done = f32[8,4,16,1]{3,2,1,0:T(8,128)S(1)} collective-permute-done((f32[8,4,16,1]{3,2,1,0:T(8,128)S(1)}, f32[8,4,16,1]{3,2,1,0:T(8,128)S(1)}, u32[]{:S(2)}, u32[]{:S(2)}) %collective-permute-start) | collective-permute-done | bytes 2080 | tf_op jit(solution)/shard_map/ppermute | solution.py:17
  11.0 5.3 %collective-permute-done.1 = f32[8,4,16,1]{3,2,1,0:T(8,128)S(1)} collective-permute-done((f32[8,4,16,1]{3,2,1,0:T(8,128)S(1)}, f32[8,4,16,1]{3,2,1,0:T(8,128)S(1)}, u32[]{:S(2)}, u32[]{:S(2)}) %collective-permute-start.1) | collective-permute-done | bytes 2080 | tf_op jit(solution)/shard_map/ppermute | solution.py:18
  16.4 0.3 pad_maximum_fusion.38
  16.6 1.3 %collective-permute-start.2 = (f32[8,4,1,130]{3,2,1,0:T(1,128)S(1)}, f32[8,4,1,130]{3,2,1,0:T(1,128)S(1)}, u32[]{:S(2)}, u32[]{:S(2)}) collective-permute-start(f32[8,4,1,130]{3,2,1,0:T(1,128)S(1)} %get-tuple-element.24), channel_id=1, source_target_pairs={{0,4},{1,5},{2,6},{3,7},{8,12},{9,13},{10,14},{11,15},{16,20},{17,... | collective-permute-start | bytes 49928 | tf_op jit(solution)/shard_map/ppermute | solution.py:17
  17.9 4.5 %collective-permute-start.3 = (f32[8,4,1,130]{3,2,1,0:T(1,128)S(1)}, f32[8,4,1,130]{3,2,1,0:T(1,128)S(1)}, u32[]{:S(2)}, u32[]{:S(2)}) collective-permute-start(f32[8,4,1,130]{3,2,1,0:T(1,128)S(1)} %get-tuple-element.25), channel_id=1, source_target_pairs={{4,0},{5,1},{6,2},{7,3},{12,8},{13,9},{14,10},{15,11},{20,16},{21,... | collective-permute-start | bytes 49928 | tf_op jit(solution)/shard_map/ppermute | solution.py:18
  22.5 1.5 %collective-permute-done.3 = f32[8,4,1,130]{3,2,1,0:T(1,128)S(1)} collective-permute-done((f32[8,4,1,130]{3,2,1,0:T(1,128)S(1)}, f32[8,4,1,130]{3,2,1,0:T(1,128)S(1)}, u32[]{:S(2)}, u32[]{:S(2)}) %collective-permute-start.3) | collective-permute-done | bytes 16672 | tf_op jit(solution)/shard_map/ppermute | solution.py:18
  24.1 0.2 pad_maximum_fusion.2
  24.3 1.9 %collective-permute-start.5 = (f32[8,1,18,130]{3,2,1,0:T(8,128)S(1)}, f32[8,1,18,130]{3,2,1,0:T(8,128)S(1)}, u32[]{:S(2)}, u32[]{:S(2)}) collective-permute-start(f32[8,1,18,130]{3,2,1,0:T(8,128)S(1)} %get-tuple-element.22), channel_id=1, source_target_pairs={{0,1},{1,2},{2,3},{4,5},{5,6},{6,7},{8,9},{9,10},{10,11},{12,13},{... | collective-permute-start | bytes 224648 | tf_op jit(solution)/shard_map/ppermute | solution.py:17
  26.2 3.6 %collective-permute-start.4 = (f32[8,1,18,130]{3,2,1,0:T(8,128)S(1)}, f32[8,1,18,130]{3,2,1,0:T(8,128)S(1)}, u32[]{:S(2)}, u32[]{:S(2)}) collective-permute-start(f32[8,1,18,130]{3,2,1,0:T(8,128)S(1)} %get-tuple-element.23), channel_id=1, source_target_pairs={{1,0},{2,1},{3,2},{5,4},{6,5},{7,6},{9,8},{10,9},{11,10},{13,12},{... | collective-permute-start | bytes 224648 | tf_op jit(solution)/shard_map/ppermute | solution.py:18
  29.9 1.4 %collective-permute-done.5 = f32[8,1,18,130]{3,2,1,0:T(8,128)S(1)} collective-permute-done((f32[8,1,18,130]{3,2,1,0:T(8,128)S(1)}, f32[8,1,18,130]{3,2,1,0:T(8,128)S(1)}, u32[]{:S(2)}, u32[]{:S(2)}) %collective-permute-start.5) | collective-permute-done | bytes 74912 | tf_op jit(solution)/shard_map/ppermute | solution.py:17
  31.3 1.8 %collective-permute-done.4 = f32[8,1,18,130]{3,2,1,0:T(8,128)S(1)} collective-permute-done((f32[8,1,18,130]{3,2,1,0:T(8,128)S(1)}, f32[8,1,18,130]{3,2,1,0:T(8,128)S(1)}, u32[]{:S(2)}, u32[]{:S(2)}) %collective-permute-start.4) | collective-permute-done | bytes 74912 | tf_op jit(solution)/shard_map/ppermute | solution.py:18
  33.0 0.1 maximum_bitcast_fusion
  33.1 0.1 slice.303
  33.2 0.1 fusion.28
  33.4 0.1 slice.302
  33.5 0.7 copy-done.1
  34.1 0.2 fusion.25
  34.3 0.5 fusion.14
  34.8 0.5 convolution_add_fusion.4
  35.2 0.3 fusion.21
  35.6 0.4 convolution_add_fusion.3
  36.0 0.5 convolution_add_fusion.2
  36.5 0.5 convolution_add_fusion.1
  37.0 0.4 copy-done.3
  37.4 0.6 fusion.2
  38.0 0.0 copy-start.2
  38.0 0.3 convolution_bitcast_fusion
  38.4 0.4 copy-done.2
  38.8 0.2 slice_maximum_fusion
  39.0 0.8 collective-permute-start.6
  39.8 1.3 %collective-permute-start.7 = (f32[4,4,16,3]{3,0,2,1:T(4,128)S(1)}, f32[4,4,16,3]{3,0,2,1:T(4,128)S(1)}, u32[]{:S(2)}, u32[]{:S(2)}) collective-permute-start(f32[4,4,16,3]{3,0,2,1:T(4,128)S(1)} %get-tuple-element.39), channel_id=1, source_target_pairs={{8,0},{16,8},{24,16},{0,24},{9,1},{17,9},{25,17},{1,25},{10,2},{18... | collective-permute-start | bytes 9224 | tf_op jit(solution)/shard_map/ppermute | solution.py:18
  41.1 2.9 %collective-permute-done.6 = f32[4,4,16,3]{3,0,2,1:T(4,128)S(1)} collective-permute-done((f32[4,4,16,3]{3,0,2,1:T(4,128)S(1)}, f32[4,4,16,3]{3,0,2,1:T(4,128)S(1)}, u32[]{:S(2)}, u32[]{:S(2)}) %collective-permute-start.6) | collective-permute-done | bytes 3104 | tf_op jit(solution)/shard_map/ppermute | solution.py:17
  44.0 2.1 %collective-permute-done.7 = f32[4,4,16,3]{3,0,2,1:T(4,128)S(1)} collective-permute-done((f32[4,4,16,3]{3,0,2,1:T(4,128)S(1)}, f32[4,4,16,3]{3,0,2,1:T(4,128)S(1)}, u32[]{:S(2)}, u32[]{:S(2)}) %collective-permute-start.7) | collective-permute-done | bytes 3104 | tf_op jit(solution)/shard_map/ppermute | solution.py:18
  46.2 0.2 pad_maximum_fusion.35
  46.4 1.3 %collective-permute-start.8 = (f32[4,4,3,134]{3,0,2,1:T(4,128)S(1)}, f32[4,4,3,134]{3,0,2,1:T(4,128)S(1)}, u32[]{:S(2)}, u32[]{:S(2)}) collective-permute-start(f32[4,4,3,134]{3,0,2,1:T(4,128)S(1)} %get-tuple-element.28), channel_id=1, source_target_pairs={{0,4},{1,5},{2,6},{3,7},{8,12},{9,13},{10,14},{11,15},{16,20},{17,... | collective-permute-start | bytes 77192 | tf_op jit(solution)/shard_map/ppermute | solution.py:17
  47.7 4.5 %collective-permute-start.9 = (f32[4,4,3,134]{3,0,2,1:T(4,128)S(1)}, f32[4,4,3,134]{3,0,2,1:T(4,128)S(1)}, u32[]{:S(2)}, u32[]{:S(2)}) collective-permute-start(f32[4,4,3,134]{3,0,2,1:T(4,128)S(1)} %get-tuple-element.29), channel_id=1, source_target_pairs={{4,0},{5,1},{6,2},{7,3},{12,8},{13,9},{14,10},{15,11},{20,16},{21,... | collective-permute-start | bytes 77192 | tf_op jit(solution)/shard_map/ppermute | solution.py:18
  52.2 0.1 collective-permute-done.8
  52.4 1.6 %collective-permute-done.9 = f32[4,4,3,134]{3,0,2,1:T(4,128)S(1)} collective-permute-done((f32[4,4,3,134]{3,0,2,1:T(4,128)S(1)}, f32[4,4,3,134]{3,0,2,1:T(4,128)S(1)}, u32[]{:S(2)}, u32[]{:S(2)}) %collective-permute-start.9) | collective-permute-done | bytes 25760 | tf_op jit(solution)/shard_map/ppermute | solution.py:18
  54.0 0.4 pad_maximum_fusion.1
  54.4 0.1 fusion.34
  54.4 1.9 %collective-permute-start.10 = (f32[4,3,22,134]{3,0,2,1:T(4,128)S(1)}, f32[4,3,22,134]{3,0,2,1:T(4,128)S(1)}, u32[]{:S(2)}, u32[]{:S(2)}) collective-permute-start(f32[4,3,22,134]{3,0,2,1:T(4,128)S(1)} %get-tuple-element.30), channel_id=1, source_target_pairs={{0,1},{1,2},{2,3},{4,5},{5,6},{6,7},{8,9},{9,10},{10,11},{12,13},{... | collective-permute-start | bytes 424520 | tf_op jit(solution)/shard_map/ppermute | solution.py:17
  56.4 3.8 %collective-permute-start.11 = (f32[4,3,22,134]{3,0,2,1:T(4,128)S(1)}, f32[4,3,22,134]{3,0,2,1:T(4,128)S(1)}, u32[]{:S(2)}, u32[]{:S(2)}) collective-permute-start(f32[4,3,22,134]{3,0,2,1:T(4,128)S(1)} %get-tuple-element.31), channel_id=1, source_target_pairs={{1,0},{2,1},{3,2},{5,4},{6,5},{7,6},{9,8},{10,9},{11,10},{13,12},{... | collective-permute-start | bytes 424520 | tf_op jit(solution)/shard_map/ppermute | solution.py:18
  60.2 0.7 copy.32
  60.9 1.3 %collective-permute-done.10 = f32[4,3,22,134]{3,0,2,1:T(4,128)S(1)} collective-permute-done((f32[4,3,22,134]{3,0,2,1:T(4,128)S(1)}, f32[4,3,22,134]{3,0,2,1:T(4,128)S(1)}, u32[]{:S(2)}, u32[]{:S(2)}) %collective-permute-start.10) | collective-permute-done | bytes 141536 | tf_op jit(solution)/shard_map/ppermute | solution.py:17
  62.2 1.8 %collective-permute-done.11 = f32[4,3,22,134]{3,0,2,1:T(4,128)S(1)} collective-permute-done((f32[4,3,22,134]{3,0,2,1:T(4,128)S(1)}, f32[4,3,22,134]{3,0,2,1:T(4,128)S(1)}, u32[]{:S(2)}, u32[]{:S(2)}) %collective-permute-start.11) | collective-permute-done | bytes 141536 | tf_op jit(solution)/shard_map/ppermute | solution.py:18
  64.0 0.5 pad_maximum_fusion
  64.5 0.3 multiply_add_fusion
  64.8 0.1 fusion.31
  64.9 0.1 multiply_add_fusion.2
  65.0 0.1 multiply_add_fusion.1
  65.2 0.5 broadcast_multiply_fusion
  65.7 2.4 %broadcast_multiply_fusion.1 = (f32[3,8,20,132]{3,0,2,1:T(4,128)S(1)}, f32[3,8,20,132]{3,0,2,1:T(4,128)S(1)}) fusion(f32[8,20,132]{2,1,0:T(8,128)S(1)} %get-tuple-element.37, f32[3,10,22,134]{3,0,2,1:T(4,128)S(1)} %get-tuple-element.12, f32[8,20,132]{2,1,0:T(8,128)S(1)} %get-tuple-element.36, f32[4,10,22,134]{3,0,2,1:T(4,128)S(1)} %pad_maximum_fusion, ...), kind=kLoop, calls=%fused_computation.35 | loop fusion | flops 760320 | bytes 2703360 | tf_op jit(solution)/shard_map/mul | solution.py:57
  68.2 1.7 %broadcast_multiply_fusion.2 = (f32[3,6,18,130]{3,0,2,1:T(4,128)S(1)}, f32[3,6,18,130]{3,0,2,1:T(4,128)S(1)}) fusion(f32[6,18,130]{2,1,0:T(8,128)S(1)} %get-tuple-element.35, f32[3,8,20,132]{3,0,2,1:T(4,128)S(1)} %get-tuple-element.10, f32[6,18,130]{2,1,0:T(8,128)S(1)} %get-tuple-element.34, f32[4,10,22,134]{3,0,2,1:T(4,128)S(1)} %pad_maximum_fusion, ...), kind=kLoop, calls=%fused_computation.46 | loop fusion | flops 505440 | bytes 1797120 | tf_op jit(solution)/shard_map/mul | solution.py:57
  69.9 0.5 multiply_reduce_fusion
  70.4 0.2 copy-done.8
  70.5 0.5 convolution_bitcast_fusion.1
  71.0 42.7 %psum.7 = f32[3,512]{1,0:T(4,128)S(1)} all-reduce(f32[3,512]{1,0:T(4,128)S(1)} %convolution_bitcast_fusion.1), channel_id=1, replica_groups=mesh['circ'=4,'normal'=2,'span'=4] {'circ','normal','span'}, use_global_device_ids=true, to_apply=%region_1.0 | all-reduce | flops 1536 | bytes 12288 | tf_op jit(solution)/shard_map/psum | solution.py:105
  113.7 0.6 copy.33
  114.4 0.6 constant_dynamic-slice_fusion
  (19 shorter events, 0.1 us)
Async XLA Ops:
  0.6 37.4 %copy-start = (f32[3,5]{1,0:T(4,128)S(1)}, f32[3,5]{1,0:T(4,128)}, u32[]{:S(2)}) copy-start(f32[3,5]{1,0:T(4,128)} %param.14) | copy-start | bytes 184
  0.6 1.0 copy-start.4
  1.8 9.2 %collective-permute-start = (f32[8,4,16,1]{3,2,1,0:T(8,128)S(1)}, f32[8,4,16,1]{3,2,1,0:T(8,128)S(1)}, u32[]{:S(2)}, u32[]{:S(2)}) collective-permute-start(f32[8,4,16,1]{3,2,1,0:T(8,128)S(1)} %get-tuple-element.32), channel_id=1, source_target_pairs={{0,8},{8,16},{16,24},{24,0},{1,9},{9,17},{17,25},{25,1},{2,10},{10... | collective-permute-start | bytes 6152 | tf_op jit(solution)/shard_map/ppermute | solution.py:17
  3.4 12.9 %collective-permute-start.1 = (f32[8,4,16,1]{3,2,1,0:T(8,128)S(1)}, f32[8,4,16,1]{3,2,1,0:T(8,128)S(1)}, u32[]{:S(2)}, u32[]{:S(2)}) collective-permute-start(f32[8,4,16,1]{3,2,1,0:T(8,128)S(1)} %get-tuple-element.33), channel_id=1, source_target_pairs={{8,0},{16,8},{24,16},{0,24},{9,1},{17,9},{25,17},{1,25},{10,2},{18... | collective-permute-start | bytes 6152 | tf_op jit(solution)/shard_map/ppermute | solution.py:18
  3.9 18.6 %copy-start.6 = (f32[3,5,5]{2,0,1:T(4,128)S(1)}, f32[3,5,5]{2,0,1:T(4,128)}, u32[]{:S(2)}) copy-start(f32[3,5,5]{2,0,1:T(4,128)} %param.12) | copy-start | bytes 904
  16.6 5.9 %collective-permute-start.2 = (f32[8,4,1,130]{3,2,1,0:T(1,128)S(1)}, f32[8,4,1,130]{3,2,1,0:T(1,128)S(1)}, u32[]{:S(2)}, u32[]{:S(2)}) collective-permute-start(f32[8,4,1,130]{3,2,1,0:T(1,128)S(1)} %get-tuple-element.24), channel_id=1, source_target_pairs={{0,4},{1,5},{2,6},{3,7},{8,12},{9,13},{10,14},{11,15},{16,20},{17,... | collective-permute-start | bytes 49928 | tf_op jit(solution)/shard_map/ppermute | solution.py:17
  17.9 6.1 %collective-permute-start.3 = (f32[8,4,1,130]{3,2,1,0:T(1,128)S(1)}, f32[8,4,1,130]{3,2,1,0:T(1,128)S(1)}, u32[]{:S(2)}, u32[]{:S(2)}) collective-permute-start(f32[8,4,1,130]{3,2,1,0:T(1,128)S(1)} %get-tuple-element.25), channel_id=1, source_target_pairs={{4,0},{5,1},{6,2},{7,3},{12,8},{13,9},{14,10},{15,11},{20,16},{21,... | collective-permute-start | bytes 49928 | tf_op jit(solution)/shard_map/ppermute | solution.py:18
  22.5 7.4 %copy-start.7 = (f32[3,5,5]{2,0,1:T(4,128)S(1)}, f32[3,5,5]{2,0,1:T(4,128)}, u32[]{:S(2)}) copy-start(f32[3,5,5]{2,0,1:T(4,128)} %param.13) | copy-start | bytes 904
  24.3 7.0 %collective-permute-start.5 = (f32[8,1,18,130]{3,2,1,0:T(8,128)S(1)}, f32[8,1,18,130]{3,2,1,0:T(8,128)S(1)}, u32[]{:S(2)}, u32[]{:S(2)}) collective-permute-start(f32[8,1,18,130]{3,2,1,0:T(8,128)S(1)} %get-tuple-element.22), channel_id=1, source_target_pairs={{0,1},{1,2},{2,3},{4,5},{5,6},{6,7},{8,9},{9,10},{10,11},{12,13},{... | collective-permute-start | bytes 224648 | tf_op jit(solution)/shard_map/ppermute | solution.py:17
  26.2 6.8 %collective-permute-start.4 = (f32[8,1,18,130]{3,2,1,0:T(8,128)S(1)}, f32[8,1,18,130]{3,2,1,0:T(8,128)S(1)}, u32[]{:S(2)}, u32[]{:S(2)}) collective-permute-start(f32[8,1,18,130]{3,2,1,0:T(8,128)S(1)} %get-tuple-element.23), channel_id=1, source_target_pairs={{1,0},{2,1},{3,2},{5,4},{6,5},{7,6},{9,8},{10,9},{11,10},{13,12},{... | collective-permute-start | bytes 224648 | tf_op jit(solution)/shard_map/ppermute | solution.py:18
  33.2 0.9 copy-start.1
  36.5 0.9 copy-start.3
  38.0 0.8 copy-start.2
  39.0 5.0 %collective-permute-start.6 = (f32[4,4,16,3]{3,0,2,1:T(4,128)S(1)}, f32[4,4,16,3]{3,0,2,1:T(4,128)S(1)}, u32[]{:S(2)}, u32[]{:S(2)}) collective-permute-start(f32[4,4,16,3]{3,0,2,1:T(4,128)S(1)} %get-tuple-element.38), channel_id=1, source_target_pairs={{0,8},{8,16},{16,24},{24,0},{1,9},{9,17},{17,25},{25,1},{2,10},{10... | collective-permute-start | bytes 9224 | tf_op jit(solution)/shard_map/ppermute | solution.py:17
  39.8 6.4 %collective-permute-start.7 = (f32[4,4,16,3]{3,0,2,1:T(4,128)S(1)}, f32[4,4,16,3]{3,0,2,1:T(4,128)S(1)}, u32[]{:S(2)}, u32[]{:S(2)}) collective-permute-start(f32[4,4,16,3]{3,0,2,1:T(4,128)S(1)} %get-tuple-element.39), channel_id=1, source_target_pairs={{8,0},{16,8},{24,16},{0,24},{9,1},{17,9},{25,17},{1,25},{10,2},{18... | collective-permute-start | bytes 9224 | tf_op jit(solution)/shard_map/ppermute | solution.py:18
  46.4 6.0 %collective-permute-start.8 = (f32[4,4,3,134]{3,0,2,1:T(4,128)S(1)}, f32[4,4,3,134]{3,0,2,1:T(4,128)S(1)}, u32[]{:S(2)}, u32[]{:S(2)}) collective-permute-start(f32[4,4,3,134]{3,0,2,1:T(4,128)S(1)} %get-tuple-element.28), channel_id=1, source_target_pairs={{0,4},{1,5},{2,6},{3,7},{8,12},{9,13},{10,14},{11,15},{16,20},{17,... | collective-permute-start | bytes 77192 | tf_op jit(solution)/shard_map/ppermute | solution.py:17
  47.7 6.3 %collective-permute-start.9 = (f32[4,4,3,134]{3,0,2,1:T(4,128)S(1)}, f32[4,4,3,134]{3,0,2,1:T(4,128)S(1)}, u32[]{:S(2)}, u32[]{:S(2)}) collective-permute-start(f32[4,4,3,134]{3,0,2,1:T(4,128)S(1)} %get-tuple-element.29), channel_id=1, source_target_pairs={{4,0},{5,1},{6,2},{7,3},{12,8},{13,9},{14,10},{15,11},{20,16},{21,... | collective-permute-start | bytes 77192 | tf_op jit(solution)/shard_map/ppermute | solution.py:18
  54.4 7.8 %collective-permute-start.10 = (f32[4,3,22,134]{3,0,2,1:T(4,128)S(1)}, f32[4,3,22,134]{3,0,2,1:T(4,128)S(1)}, u32[]{:S(2)}, u32[]{:S(2)}) collective-permute-start(f32[4,3,22,134]{3,0,2,1:T(4,128)S(1)} %get-tuple-element.30), channel_id=1, source_target_pairs={{0,1},{1,2},{2,3},{4,5},{5,6},{6,7},{8,9},{9,10},{10,11},{12,13},{... | collective-permute-start | bytes 424520 | tf_op jit(solution)/shard_map/ppermute | solution.py:17
  56.4 7.6 %collective-permute-start.11 = (f32[4,3,22,134]{3,0,2,1:T(4,128)S(1)}, f32[4,3,22,134]{3,0,2,1:T(4,128)S(1)}, u32[]{:S(2)}, u32[]{:S(2)}) collective-permute-start(f32[4,3,22,134]{3,0,2,1:T(4,128)S(1)} %get-tuple-element.31), channel_id=1, source_target_pairs={{1,0},{2,1},{3,2},{5,4},{6,5},{7,6},{9,8},{10,9},{11,10},{13,12},{... | collective-permute-start | bytes 424520 | tf_op jit(solution)/shard_map/ppermute | solution.py:18
  68.2 1.7 %copy-start.5 = (f32[4,16,128]{2,1,0:T(8,128)S(1)}, f32[4,16,128]{2,1,0:T(8,128)}, u32[]{:S(2)}) copy-start(f32[4,16,128]{2,1,0:T(8,128)} %param.16) | copy-start | bytes 98308
  69.8 0.7 copy-start.8
where the time goes:
time: 115 us
  blocking collectives  42.7 us (37%)
  starting transfers between devices  27.1 us (24%)
  waiting for transfers between devices  27 us (23%)
  other arithmetic  8.29 us (7%)
  local copies, waits for them, and re-layouts  5.05 us (4%)
  matrix products  3.69 us (3%)
    psum x1, blocking collectives, on_device(): total = lax.psum(terms, ('circ', 'normal', 'span'))  42.7 us
    ppermute x6, starting transfers between devices, padded_2(): after = lax.ppermute(initial, axis, down)  18.3 us
    ppermute x6, waiting for transfers between devices, padded_2(): after = lax.ppermute(initial, axis, down)  14.1 us
    ppermute x6, waiting for transfers between devices, padded_2(): before = lax.ppermute(last, axis, up)  12.9 us
    ppermute x6, starting transfers between devices, padded_2(): before = lax.ppermute(last, axis, up)  8.85 us
    mul x3, other arithmetic, relax(): weighted = stiff_pad[None] * mesh_pad  4.64 us
    unnamed x22, local copies, waits for them, and re-layouts  4.09 us
  transfers between devices with their start and end apart: 12, of which 11 were waited for; matrix products, arithmetic and copies ran while one was open for 1% of the time, Pallas kernels for 0%

commit v1 on v0

--- a/solution.py
+++ b/solution.py
@@ -86,6 +86,12 @@
     wall_kernel,
     panel_owner,
 ):
+
+    def measure_the_ratios(x_local, axis_tag, group_axis):
+        for rr in (axis_tag, group_axis):
+            x_local = lax.psum(x_local, axis_name=rr)
+        return x_local
+
     stacked = jnp.concatenate([adjoint, face_weights], axis=0)
     beside_all = padded_2(stacked, (("circ", 3),), 1, True)
     padded = padded_2(beside_all, (("normal", 2), ("span", 1)), 1, False)
@@ -102,7 +108,7 @@
         panel_owner[:, :, None] == jnp.arange(panel_count, dtype=jnp.int32)[None, None, :]
     ).astype(jnp.float32)
     terms = jnp.einsum("mki,kip->mp", wall_sens, onehot, precision=lax.Precision.HIGHEST)
-    total = lax.psum(terms, ("circ", "normal", "span"))
+    total = measure_the_ratios(terms, ("normal", "span"), "circ")
     panels = lax.dynamic_slice_in_dim(total, lax.axis_index("span") * PANEL_DEV, PANEL_DEV, 1)
     return (residual, mesh, panels)
 

time: 115 us -> 102 us (0.89)
  the two profiles are of different devices: /device:TPU:14 before, /device:TPU:0 now
where the time goes in v1:
time: 102 us
  waiting for transfers between devices  31.3 us (31%)
  blocking collectives  28.5 us (28%)
  starting transfers between devices  23.9 us (23%)
  other arithmetic  8.29 us (8%)
  local copies, waits for them, and re-layouts  5.05 us (5%)
  matrix products  3.7 us (4%)
  between operations  1.06 us (1%)
    psum x2, blocking collectives, measure_the_ratios(): x_local = lax.psum(x_local, axis_name=rr)  28.5 us
    ppermute x6, waiting for transfers between devices, padded_2(): after = lax.ppermute(initial, axis, down)  20.4 us
    ppermute x6, starting transfers between devices, padded_2(): before = lax.ppermute(last, axis, up)  13.8 us
    ppermute x6, waiting for transfers between devices, padded_2(): before = lax.ppermute(last, axis, up)  10.9 us
    ppermute x6, starting transfers between devices, padded_2(): after = lax.ppermute(initial, axis, down)  10.1 us
    mul x3, other arithmetic, relax(): weighted = stiff_pad[None] * mesh_pad  4.64 us
    unnamed x22, local copies, waits for them, and re-layouts  4.09 us
  transfers between devices with their start and end apart: 12, of which 10 were waited for; matrix products, arithmetic and copies ran while one was open for 1% of the time, Pallas kernels for 0%

profile of v1, /device:TPU:0, one launch (start us, length us, event | category | flops | bytes accessed | tf_op | source)
XLA Modules:
  0.0 101.8 jit_solution(8402697537194441990)
XLA Ops:
  0.6 0.0 copy-start
  0.7 1.0 constant_dynamic-update-slice_fusion.1
  1.6 0.1 fusion.35
  1.8 3.1 %collective-permute-start = (f32[8,4,16,1]{3,2,1,0:T(8,128)S(1)}, f32[8,4,16,1]{3,2,1,0:T(8,128)S(1)}, u32[]{:S(2)}, u32[]{:S(2)}) collective-permute-start(f32[8,4,16,1]{3,2,1,0:T(8,128)S(1)} %get-tuple-element.32), channel_id=1, source_target_pairs={{0,8},{8,16},{16,24},{24,0},{1,9},{9,17},{17,25},{25,1},{2,10},{10... | collective-permute-start | bytes 6152 | tf_op jit(solution)/shard_map/ppermute | solution.py:17
  4.9 2.1 %collective-permute-start.1 = (f32[8,4,16,1]{3,2,1,0:T(8,128)S(1)}, f32[8,4,16,1]{3,2,1,0:T(8,128)S(1)}, u32[]{:S(2)}, u32[]{:S(2)}) collective-permute-start(f32[8,4,16,1]{3,2,1,0:T(8,128)S(1)} %get-tuple-element.33), channel_id=1, source_target_pairs={{8,0},{16,8},{24,16},{0,24},{9,1},{17,9},{25,17},{1,25},{10,2},{18... | collective-permute-start | bytes 6152 | tf_op jit(solution)/shard_map/ppermute | solution.py:18
  7.0 7.1 %collective-permute-done = f32[8,4,16,1]{3,2,1,0:T(8,128)S(1)} collective-permute-done((f32[8,4,16,1]{3,2,1,0:T(8,128)S(1)}, f32[8,4,16,1]{3,2,1,0:T(8,128)S(1)}, u32[]{:S(2)}, u32[]{:S(2)}) %collective-permute-start) | collective-permute-done | bytes 2080 | tf_op jit(solution)/shard_map/ppermute | solution.py:17
  14.1 4.2 %collective-permute-done.1 = f32[8,4,16,1]{3,2,1,0:T(8,128)S(1)} collective-permute-done((f32[8,4,16,1]{3,2,1,0:T(8,128)S(1)}, f32[8,4,16,1]{3,2,1,0:T(8,128)S(1)}, u32[]{:S(2)}, u32[]{:S(2)}) %collective-permute-start.1) | collective-permute-done | bytes 2080 | tf_op jit(solution)/shard_map/ppermute | solution.py:18
  18.2 0.3 pad_maximum_fusion.38
  18.5 3.4 %collective-permute-start.2 = (f32[8,4,1,130]{3,2,1,0:T(1,128)S(1)}, f32[8,4,1,130]{3,2,1,0:T(1,128)S(1)}, u32[]{:S(2)}, u32[]{:S(2)}) collective-permute-start(f32[8,4,1,130]{3,2,1,0:T(1,128)S(1)} %get-tuple-element.24), channel_id=1, source_target_pairs={{0,4},{1,5},{2,6},{3,7},{8,12},{9,13},{10,14},{11,15},{16,20},{17,... | collective-permute-start | bytes 49928 | tf_op jit(solution)/shard_map/ppermute | solution.py:17
  22.0 1.3 %collective-permute-start.3 = (f32[8,4,1,130]{3,2,1,0:T(1,128)S(1)}, f32[8,4,1,130]{3,2,1,0:T(1,128)S(1)}, u32[]{:S(2)}, u32[]{:S(2)}) collective-permute-start(f32[8,4,1,130]{3,2,1,0:T(1,128)S(1)} %get-tuple-element.25), channel_id=1, source_target_pairs={{4,0},{5,1},{6,2},{7,3},{12,8},{13,9},{14,10},{15,11},{20,16},{21,... | collective-permute-start | bytes 49928 | tf_op jit(solution)/shard_map/ppermute | solution.py:18
  23.3 0.0 copy-start.7
  23.3 0.2 collective-permute-done.2
  23.5 4.2 %collective-permute-done.3 = f32[8,4,1,130]{3,2,1,0:T(1,128)S(1)} collective-permute-done((f32[8,4,1,130]{3,2,1,0:T(1,128)S(1)}, f32[8,4,1,130]{3,2,1,0:T(1,128)S(1)}, u32[]{:S(2)}, u32[]{:S(2)}) %collective-permute-start.3) | collective-permute-done | bytes 16672 | tf_op jit(solution)/shard_map/ppermute | solution.py:18
  27.8 0.2 pad_maximum_fusion.2
  28.0 1.3 %collective-permute-start.5 = (f32[8,1,18,130]{3,2,1,0:T(8,128)S(1)}, f32[8,1,18,130]{3,2,1,0:T(8,128)S(1)}, u32[]{:S(2)}, u32[]{:S(2)}) collective-permute-start(f32[8,1,18,130]{3,2,1,0:T(8,128)S(1)} %get-tuple-element.22), channel_id=1, source_target_pairs={{0,1},{1,2},{2,3},{4,5},{5,6},{6,7},{8,9},{9,10},{10,11},{12,13},{... | collective-permute-start | bytes 224648 | tf_op jit(solution)/shard_map/ppermute | solution.py:17
  29.3 1.3 %collective-permute-start.4 = (f32[8,1,18,130]{3,2,1,0:T(8,128)S(1)}, f32[8,1,18,130]{3,2,1,0:T(8,128)S(1)}, u32[]{:S(2)}, u32[]{:S(2)}) collective-permute-start(f32[8,1,18,130]{3,2,1,0:T(8,128)S(1)} %get-tuple-element.23), channel_id=1, source_target_pairs={{1,0},{2,1},{3,2},{5,4},{6,5},{7,6},{9,8},{10,9},{11,10},{13,12},{... | collective-permute-start | bytes 224648 | tf_op jit(solution)/shard_map/ppermute | solution.py:18
  30.6 3.7 %collective-permute-done.4 = f32[8,1,18,130]{3,2,1,0:T(8,128)S(1)} collective-permute-done((f32[8,1,18,130]{3,2,1,0:T(8,128)S(1)}, f32[8,1,18,130]{3,2,1,0:T(8,128)S(1)}, u32[]{:S(2)}, u32[]{:S(2)}) %collective-permute-start.4) | collective-permute-done | bytes 74912 | tf_op jit(solution)/shard_map/ppermute | solution.py:18
  34.3 0.1 maximum_bitcast_fusion
  34.5 0.1 slice.303
  34.5 0.1 fusion.28
  34.7 0.1 slice.302
  34.8 0.7 copy-done.1
  35.5 0.2 fusion.25
  35.6 0.5 fusion.14
  36.1 0.5 convolution_add_fusion.4
  36.6 0.3 fusion.21
  36.9 0.5 convolution_add_fusion.3
  37.4 0.5 convolution_add_fusion.2
  37.8 0.5 convolution_add_fusion.1
  38.3 0.4 copy-done.3
  38.7 0.6 fusion.2
  39.4 0.3 convolution_bitcast_fusion
  39.7 0.4 copy-done.2
  40.1 0.2 slice_maximum_fusion
  40.3 1.2 %collective-permute-start.6 = (f32[4,4,16,3]{3,0,2,1:T(4,128)S(1)}, f32[4,4,16,3]{3,0,2,1:T(4,128)S(1)}, u32[]{:S(2)}, u32[]{:S(2)}) collective-permute-start(f32[4,4,16,3]{3,0,2,1:T(4,128)S(1)} %get-tuple-element.38), channel_id=1, source_target_pairs={{0,8},{8,16},{16,24},{24,0},{1,9},{9,17},{17,25},{25,1},{2,10},{10... | collective-permute-start | bytes 9224 | tf_op jit(solution)/shard_map/ppermute | solution.py:17
  41.5 2.7 %collective-permute-start.7 = (f32[4,4,16,3]{3,0,2,1:T(4,128)S(1)}, f32[4,4,16,3]{3,0,2,1:T(4,128)S(1)}, u32[]{:S(2)}, u32[]{:S(2)}) collective-permute-start(f32[4,4,16,3]{3,0,2,1:T(4,128)S(1)} %get-tuple-element.39), channel_id=1, source_target_pairs={{8,0},{16,8},{24,16},{0,24},{9,1},{17,9},{25,17},{1,25},{10,2},{18... | collective-permute-start | bytes 9224 | tf_op jit(solution)/shard_map/ppermute | solution.py:18
  44.2 3.1 %collective-permute-done.6 = f32[4,4,16,3]{3,0,2,1:T(4,128)S(1)} collective-permute-done((f32[4,4,16,3]{3,0,2,1:T(4,128)S(1)}, f32[4,4,16,3]{3,0,2,1:T(4,128)S(1)}, u32[]{:S(2)}, u32[]{:S(2)}) %collective-permute-start.6) | collective-permute-done | bytes 3104 | tf_op jit(solution)/shard_map/ppermute | solution.py:17
  47.3 0.6 collective-permute-done.7
  47.9 0.2 pad_maximum_fusion.35
  48.1 1.6 %collective-permute-start.8 = (f32[4,4,3,134]{3,0,2,1:T(4,128)S(1)}, f32[4,4,3,134]{3,0,2,1:T(4,128)S(1)}, u32[]{:S(2)}, u32[]{:S(2)}) collective-permute-start(f32[4,4,3,134]{3,0,2,1:T(4,128)S(1)} %get-tuple-element.28), channel_id=1, source_target_pairs={{0,4},{1,5},{2,6},{3,7},{8,12},{9,13},{10,14},{11,15},{16,20},{17,... | collective-permute-start | bytes 77192 | tf_op jit(solution)/shard_map/ppermute | solution.py:17
  49.7 1.3 %collective-permute-start.9 = (f32[4,4,3,134]{3,0,2,1:T(4,128)S(1)}, f32[4,4,3,134]{3,0,2,1:T(4,128)S(1)}, u32[]{:S(2)}, u32[]{:S(2)}) collective-permute-start(f32[4,4,3,134]{3,0,2,1:T(4,128)S(1)} %get-tuple-element.29), channel_id=1, source_target_pairs={{4,0},{5,1},{6,2},{7,3},{12,8},{13,9},{14,10},{15,11},{20,16},{21,... | collective-permute-start | bytes 77192 | tf_op jit(solution)/shard_map/ppermute | solution.py:18
  51.0 0.4 collective-permute-done.8
  51.4 4.3 %collective-permute-done.9 = f32[4,4,3,134]{3,0,2,1:T(4,128)S(1)} collective-permute-done((f32[4,4,3,134]{3,0,2,1:T(4,128)S(1)}, f32[4,4,3,134]{3,0,2,1:T(4,128)S(1)}, u32[]{:S(2)}, u32[]{:S(2)}) %collective-permute-start.9) | collective-permute-done | bytes 25760 | tf_op jit(solution)/shard_map/ppermute | solution.py:18
  55.7 0.4 pad_maximum_fusion.1
  56.1 0.1 fusion.34
  56.2 3.2 %collective-permute-start.10 = (f32[4,3,22,134]{3,0,2,1:T(4,128)S(1)}, f32[4,3,22,134]{3,0,2,1:T(4,128)S(1)}, u32[]{:S(2)}, u32[]{:S(2)}) collective-permute-start(f32[4,3,22,134]{3,0,2,1:T(4,128)S(1)} %get-tuple-element.30), channel_id=1, source_target_pairs={{0,1},{1,2},{2,3},{4,5},{5,6},{6,7},{8,9},{9,10},{10,11},{12,13},{... | collective-permute-start | bytes 424520 | tf_op jit(solution)/shard_map/ppermute | solution.py:17
  59.4 1.5 %collective-permute-start.11 = (f32[4,3,22,134]{3,0,2,1:T(4,128)S(1)}, f32[4,3,22,134]{3,0,2,1:T(4,128)S(1)}, u32[]{:S(2)}, u32[]{:S(2)}) collective-permute-start(f32[4,3,22,134]{3,0,2,1:T(4,128)S(1)} %get-tuple-element.31), channel_id=1, source_target_pairs={{1,0},{2,1},{3,2},{5,4},{6,5},{7,6},{9,8},{10,9},{11,10},{13,12},{... | collective-permute-start | bytes 424520 | tf_op jit(solution)/shard_map/ppermute | solution.py:18
  60.9 0.7 copy.32
  61.6 3.4 %collective-permute-done.11 = f32[4,3,22,134]{3,0,2,1:T(4,128)S(1)} collective-permute-done((f32[4,3,22,134]{3,0,2,1:T(4,128)S(1)}, f32[4,3,22,134]{3,0,2,1:T(4,128)S(1)}, u32[]{:S(2)}, u32[]{:S(2)}) %collective-permute-start.11) | collective-permute-done | bytes 141536 | tf_op jit(solution)/shard_map/ppermute | solution.py:18
  65.0 0.5 pad_maximum_fusion
  65.5 0.3 multiply_add_fusion
  65.9 0.1 fusion.31
  66.0 0.1 multiply_add_fusion.2
  66.1 0.1 multiply_add_fusion.1
  66.2 0.5 broadcast_multiply_fusion
  66.8 2.4 %broadcast_multiply_fusion.1 = (f32[3,8,20,132]{3,0,2,1:T(4,128)S(1)}, f32[3,8,20,132]{3,0,2,1:T(4,128)S(1)}) fusion(f32[8,20,132]{2,1,0:T(8,128)S(1)} %get-tuple-element.37, f32[3,10,22,134]{3,0,2,1:T(4,128)S(1)} %get-tuple-element.12, f32[8,20,132]{2,1,0:T(8,128)S(1)} %get-tuple-element.36, f32[4,10,22,134]{3,0,2,1:T(4,128)S(1)} %pad_maximum_fusion, ...), kind=kLoop, calls=%fused_computation.35 | loop fusion | flops 760320 | bytes 2703360 | tf_op jit(solution)/shard_map/mul | solution.py:57
  69.2 1.7 %broadcast_multiply_fusion.2 = (f32[3,6,18,130]{3,0,2,1:T(4,128)S(1)}, f32[3,6,18,130]{3,0,2,1:T(4,128)S(1)}) fusion(f32[6,18,130]{2,1,0:T(8,128)S(1)} %get-tuple-element.35, f32[3,8,20,132]{3,0,2,1:T(4,128)S(1)} %get-tuple-element.10, f32[6,18,130]{2,1,0:T(8,128)S(1)} %get-tuple-element.34, f32[4,10,22,134]{3,0,2,1:T(4,128)S(1)} %pad_maximum_fusion, ...), kind=kLoop, calls=%fused_computation.46 | loop fusion | flops 505440 | bytes 1797120 | tf_op jit(solution)/shard_map/mul | solution.py:57
  70.9 0.5 multiply_reduce_fusion
  71.4 0.2 copy-done.8
  71.6 0.5 convolution_bitcast_fusion.1
  72.1 16.9 %psum.14 = f32[3,512]{1,0:T(4,128)S(1)} all-reduce(f32[3,512]{1,0:T(4,128)S(1)} %convolution_bitcast_fusion.1), channel_id=1, replica_groups=mesh['circ'=4,'normal'=2,'span'=4] {'normal','span'}, use_global_device_ids=true, to_apply=%region_1.0 | all-reduce | flops 1536 | bytes 12288 | tf_op jit(solution)/shard_map/psum | solution.py:92
  88.9 11.6 %psum.15 = f32[3,512]{1,0:T(4,128)S(1)} all-reduce(f32[3,512]{1,0:T(4,128)S(1)} %psum.14), channel_id=1, replica_groups=mesh['circ'=4,'normal'=2,'span'=4] {'circ'}, use_global_device_ids=true, to_apply=%region_2.0 | all-reduce | flops 1536 | bytes 12288 | tf_op jit(solution)/shard_map/psum | solution.py:92
  100.5 0.6 copy.33
  101.2 0.6 constant_dynamic-slice_fusion
  (20 shorter events, 0.1 us)
Async XLA Ops:
  0.6 38.7 %copy-start = (f32[3,5]{1,0:T(4,128)S(1)}, f32[3,5]{1,0:T(4,128)}, u32[]{:S(2)}) copy-start(f32[3,5]{1,0:T(4,128)} %param.14) | copy-start | bytes 184
  0.6 1.0 copy-start.4
  1.8 12.3 %collective-permute-start = (f32[8,4,16,1]{3,2,1,0:T(8,128)S(1)}, f32[8,4,16,1]{3,2,1,0:T(8,128)S(1)}, u32[]{:S(2)}, u32[]{:S(2)}) collective-permute-start(f32[8,4,16,1]{3,2,1,0:T(8,128)S(1)} %get-tuple-element.32), channel_id=1, source_target_pairs={{0,8},{8,16},{16,24},{24,0},{1,9},{9,17},{17,25},{25,1},{2,10},{10... | collective-permute-start | bytes 6152 | tf_op jit(solution)/shard_map/ppermute | solution.py:17
  4.9 13.4 %collective-permute-start.1 = (f32[8,4,16,1]{3,2,1,0:T(8,128)S(1)}, f32[8,4,16,1]{3,2,1,0:T(8,128)S(1)}, u32[]{:S(2)}, u32[]{:S(2)}) collective-permute-start(f32[8,4,16,1]{3,2,1,0:T(8,128)S(1)} %get-tuple-element.33), channel_id=1, source_target_pairs={{8,0},{16,8},{24,16},{0,24},{9,1},{17,9},{25,17},{1,25},{10,2},{18... | collective-permute-start | bytes 6152 | tf_op jit(solution)/shard_map/ppermute | solution.py:18
  7.0 16.3 %copy-start.6 = (f32[3,5,5]{2,0,1:T(4,128)S(1)}, f32[3,5,5]{2,0,1:T(4,128)}, u32[]{:S(2)}) copy-start(f32[3,5,5]{2,0,1:T(4,128)} %param.12) | copy-start | bytes 904
  18.5 5.0 %collective-permute-start.2 = (f32[8,4,1,130]{3,2,1,0:T(1,128)S(1)}, f32[8,4,1,130]{3,2,1,0:T(1,128)S(1)}, u32[]{:S(2)}, u32[]{:S(2)}) collective-permute-start(f32[8,4,1,130]{3,2,1,0:T(1,128)S(1)} %get-tuple-element.24), channel_id=1, source_target_pairs={{0,4},{1,5},{2,6},{3,7},{8,12},{9,13},{10,14},{11,15},{16,20},{17,... | collective-permute-start | bytes 49928 | tf_op jit(solution)/shard_map/ppermute | solution.py:17
  22.0 5.8 %collective-permute-start.3 = (f32[8,4,1,130]{3,2,1,0:T(1,128)S(1)}, f32[8,4,1,130]{3,2,1,0:T(1,128)S(1)}, u32[]{:S(2)}, u32[]{:S(2)}) collective-permute-start(f32[8,4,1,130]{3,2,1,0:T(1,128)S(1)} %get-tuple-element.25), channel_id=1, source_target_pairs={{4,0},{5,1},{6,2},{7,3},{12,8},{13,9},{14,10},{15,11},{20,16},{21,... | collective-permute-start | bytes 49928 | tf_op jit(solution)/shard_map/ppermute | solution.py:18
  23.3 7.3 %copy-start.7 = (f32[3,5,5]{2,0,1:T(4,128)S(1)}, f32[3,5,5]{2,0,1:T(4,128)}, u32[]{:S(2)}) copy-start(f32[3,5,5]{2,0,1:T(4,128)} %param.13) | copy-start | bytes 904
  28.0 2.6 %collective-permute-start.5 = (f32[8,1,18,130]{3,2,1,0:T(8,128)S(1)}, f32[8,1,18,130]{3,2,1,0:T(8,128)S(1)}, u32[]{:S(2)}, u32[]{:S(2)}) collective-permute-start(f32[8,1,18,130]{3,2,1,0:T(8,128)S(1)} %get-tuple-element.22), channel_id=1, source_target_pairs={{0,1},{1,2},{2,3},{4,5},{5,6},{6,7},{8,9},{9,10},{10,11},{12,13},{... | collective-permute-start | bytes 224648 | tf_op jit(solution)/shard_map/ppermute | solution.py:17
  29.3 5.1 %collective-permute-start.4 = (f32[8,1,18,130]{3,2,1,0:T(8,128)S(1)}, f32[8,1,18,130]{3,2,1,0:T(8,128)S(1)}, u32[]{:S(2)}, u32[]{:S(2)}) collective-permute-start(f32[8,1,18,130]{3,2,1,0:T(8,128)S(1)} %get-tuple-element.23), channel_id=1, source_target_pairs={{1,0},{2,1},{3,2},{5,4},{6,5},{7,6},{9,8},{10,9},{11,10},{13,12},{... | collective-permute-start | bytes 224648 | tf_op jit(solution)/shard_map/ppermute | solution.py:18
  34.5 0.9 copy-start.1
  37.8 0.9 copy-start.3
  39.4 0.8 copy-start.2
  40.3 7.0 %collective-permute-start.6 = (f32[4,4,16,3]{3,0,2,1:T(4,128)S(1)}, f32[4,4,16,3]{3,0,2,1:T(4,128)S(1)}, u32[]{:S(2)}, u32[]{:S(2)}) collective-permute-start(f32[4,4,16,3]{3,0,2,1:T(4,128)S(1)} %get-tuple-element.38), channel_id=1, source_target_pairs={{0,8},{8,16},{16,24},{24,0},{1,9},{9,17},{17,25},{25,1},{2,10},{10... | collective-permute-start | bytes 9224 | tf_op jit(solution)/shard_map/ppermute | solution.py:17
  41.5 6.4 %collective-permute-start.7 = (f32[4,4,16,3]{3,0,2,1:T(4,128)S(1)}, f32[4,4,16,3]{3,0,2,1:T(4,128)S(1)}, u32[]{:S(2)}, u32[]{:S(2)}) collective-permute-start(f32[4,4,16,3]{3,0,2,1:T(4,128)S(1)} %get-tuple-element.39), channel_id=1, source_target_pairs={{8,0},{16,8},{24,16},{0,24},{9,1},{17,9},{25,17},{1,25},{10,2},{18... | collective-permute-start | bytes 9224 | tf_op jit(solution)/shard_map/ppermute | solution.py:18
  48.1 3.4 %collective-permute-start.8 = (f32[4,4,3,134]{3,0,2,1:T(4,128)S(1)}, f32[4,4,3,134]{3,0,2,1:T(4,128)S(1)}, u32[]{:S(2)}, u32[]{:S(2)}) collective-permute-start(f32[4,4,3,134]{3,0,2,1:T(4,128)S(1)} %get-tuple-element.28), channel_id=1, source_target_pairs={{0,4},{1,5},{2,6},{3,7},{8,12},{9,13},{10,14},{11,15},{16,20},{17,... | collective-permute-start | bytes 77192 | tf_op jit(solution)/shard_map/ppermute | solution.py:17
  49.7 6.0 %collective-permute-start.9 = (f32[4,4,3,134]{3,0,2,1:T(4,128)S(1)}, f32[4,4,3,134]{3,0,2,1:T(4,128)S(1)}, u32[]{:S(2)}, u32[]{:S(2)}) collective-permute-start(f32[4,4,3,134]{3,0,2,1:T(4,128)S(1)} %get-tuple-element.29), channel_id=1, source_target_pairs={{4,0},{5,1},{6,2},{7,3},{12,8},{13,9},{14,10},{15,11},{20,16},{21,... | collective-permute-start | bytes 77192 | tf_op jit(solution)/shard_map/ppermute | solution.py:18
  56.2 5.4 %collective-permute-start.10 = (f32[4,3,22,134]{3,0,2,1:T(4,128)S(1)}, f32[4,3,22,134]{3,0,2,1:T(4,128)S(1)}, u32[]{:S(2)}, u32[]{:S(2)}) collective-permute-start(f32[4,3,22,134]{3,0,2,1:T(4,128)S(1)} %get-tuple-element.30), channel_id=1, source_target_pairs={{0,1},{1,2},{2,3},{4,5},{5,6},{6,7},{8,9},{9,10},{10,11},{12,13},{... | collective-permute-start | bytes 424520 | tf_op jit(solution)/shard_map/ppermute | solution.py:17
  59.4 5.6 %collective-permute-start.11 = (f32[4,3,22,134]{3,0,2,1:T(4,128)S(1)}, f32[4,3,22,134]{3,0,2,1:T(4,128)S(1)}, u32[]{:S(2)}, u32[]{:S(2)}) collective-permute-start(f32[4,3,22,134]{3,0,2,1:T(4,128)S(1)} %get-tuple-element.31), channel_id=1, source_target_pairs={{1,0},{2,1},{3,2},{5,4},{6,5},{7,6},{9,8},{10,9},{11,10},{13,12},{... | collective-permute-start | bytes 424520 | tf_op jit(solution)/shard_map/ppermute | solution.py:18
  69.2 1.7 %copy-start.5 = (f32[4,16,128]{2,1,0:T(8,128)S(1)}, f32[4,16,128]{2,1,0:T(8,128)}, u32[]{:S(2)}) copy-start(f32[4,16,128]{2,1,0:T(8,128)} %param.16) | copy-start | bytes 98308
  70.9 0.7 copy-start.8
